TPU v7x, 128 devices: a whole 4x4x4 slice. The times are simulated.
128 devices in a mesh: row: 8 (over y, core), col: 16 (over z, x).
Axes of the slice: x: 4, y: 4, z: 4, core: 2. Of those that a mesh axis runs over, the one named last changes fastest.
Arguments:
- fock: bfloat16 [32768, 16, 2048], P('row', 'col'), may hold values from -6 to 6
- lmo_coef: bfloat16 [32768, 1024], P(('row', 'col')), may hold values from -0.078125 to 0.078125
- three_index: bfloat16 [32768, 512], P(('row', 'col')), may hold values from -6 to 6
- rotation: bfloat16 [16, 8, 1024, 512], P('col', 'row'), may hold values from -0.1875 to 0.1875
- lmo_ids: int32 [16, 8], replicated, may hold values from 0 to 127, as said below
- domains: int32 [128, 8], replicated, may hold values from -1 to 255, as said below
Outputs:
- proj_fock: float32 [16, 8, 512, 512], P('col', 'row')
- three_rot: bfloat16 [16, 8, 512, 512], P('col', 'row')
Inputs may be any that keep to these rules, and one draw needn't show every extreme that they name: `lmo_ids`: every LMO number appears exactly once; row o lists the 8 LMOs owned by column set o. `domains`: entry k of a list is -1 or a block of row panel k; entry 0 is never -1. The present blocks of one list lie in distinct column sets. For one owner o and one entry k, the blocks of the lists of lmo_ids[o, j] over all j lie in distinct column sets; for one j and one entry k, those of lmo_ids[o, j] over all o do too.
All inputs are finite; a program needn't handle non-finite values.
Results may differ from a plain program's by a relative error of at most 0.02.
Values may be sent and summed in bfloat16 or wider, within the bound.
No kernel may reach another device: no remote copies, remote signals or barrier semaphores. Data moves between devices by JAX's collectives and lax.ppermute only.
A program may use at most 192 MiB of HBM per device.

v0:
```python
import jax
import jax.numpy as jnp
from jax import lax
from jax.sharding import PartitionSpec as P

BLK = 128


def locate(blocks, dev_blocks, num_sets):
    present = blocks >= 0
    clipped = jnp.maximum(blocks, 0)
    flat_dev = clipped // dev_blocks
    return (present, flat_dev % num_sets, flat_dev // num_sets, clipped % dev_blocks)


def body(fock, lmo_coef, three_index, rotation, lmo_ids, domains):
    num_panels = lax.axis_size("row")
    num_sets = lax.axis_size("col")
    my_row = lax.axis_index("row")
    my_col = lax.axis_index("col")
    dev_rows = lmo_coef.shape[0]
    occ_width = lmo_coef.shape[1]
    dev_blocks = dev_rows // BLK
    dom_blocks = domains.shape[1]
    per_panel = dom_blocks // num_panels
    dev_lmos = rotation.shape[1]
    dom_width = dom_blocks * BLK
    panel_fock = fock[:, 0, :]
    gathered = lax.all_gather(lmo_coef, "row", axis=0, tiled=True)
    fock_coef = lax.psum_scatter(
        jnp.dot(panel_fock, gathered, preferred_element_type=jnp.float32).astype(jnp.bfloat16),
        "col",
        scatter_dimension=0,
        tiled=True,
    ).astype(jnp.float32)
    occ_term = jnp.einsum(
        "ri,rj->ij", lmo_coef, fock_coef.astype(jnp.bfloat16), preferred_element_type=jnp.float32
    )
    occ_fock = lax.psum(occ_term, ("row", "col"))
    correction = jnp.dot(
        lmo_coef, occ_fock.astype(jnp.bfloat16), preferred_element_type=jnp.float32
    )
    proj_rows = (fock_coef - 0.5 * correction).astype(jnp.bfloat16)
    all_rows = jnp.concatenate([lmo_coef, proj_rows, three_index], axis=1)
    row_width = all_rows.shape[1]
    row_blocks = all_rows.reshape(dev_blocks, BLK, row_width)
    fock_tiles = panel_fock.reshape(num_sets * dev_blocks, BLK, num_panels * dev_blocks, BLK)
    owner_doms = jnp.take(domains, lmo_ids, axis=0)
    present, col_set, panel_id, sub_block = locate(owner_doms, dev_blocks, num_sets)
    row_tile = col_set * dev_blocks + sub_block
    col_tile = panel_id * dev_blocks + sub_block
    holds_col = present & (col_set == my_col)
    my_col_tile = jnp.sum(jnp.where(holds_col, col_tile, 0), axis=2)
    has_col = jnp.any(holds_col, axis=2)
    sub_range = jnp.arange(dev_blocks, dtype=jnp.int32)
    set_range = jnp.arange(num_sets, dtype=jnp.int32)
    slot_start = my_row * per_panel
    mine_slot = lax.dynamic_slice_in_dim(holds_col, slot_start, per_panel, 2)
    sub_slot = lax.dynamic_slice_in_dim(sub_block, slot_start, per_panel, 2)
    row_slot = lax.dynamic_slice_in_dim(row_tile, slot_start, per_panel, 2)
    live_slot = lax.dynamic_slice_in_dim(present, slot_start, per_panel, 2) & has_col[:, :, None]
    owner_present = lax.dynamic_index_in_dim(present, my_col, 0, keepdims=False)
    owner_sets = lax.dynamic_index_in_dim(col_set, my_col, 0, keepdims=False)
    pick_rows = (mine_slot[..., None] & (sub_slot[..., None] == sub_range)).astype(jnp.bfloat16)
    rows_out = jnp.einsum(
        "ojps,sbw->opbw", pick_rows, row_blocks, preferred_element_type=jnp.float32
    ).astype(jnp.bfloat16)
    tiles_out = fock_tiles[row_slot, :, my_col_tile[:, :, None], :]
    tiles_out = jnp.where(live_slot[..., None, None], tiles_out, jnp.zeros_like(tiles_out))
    got_rows, got_tiles = (
        lax.all_to_all(rows_out, "col", split_axis=0, concat_axis=0, tiled=True),
        lax.all_to_all(tiles_out, "col", split_axis=0, concat_axis=0, tiled=True),
    )
    source = ((owner_sets[..., None] == set_range) & owner_present[..., None]).astype(jnp.bfloat16)
    source_slot = lax.dynamic_slice_in_dim(source, slot_start, per_panel, 1)
    source_slot = source_slot.reshape(num_panels, dev_lmos, per_panel, num_sets)
    strip_rows = jnp.einsum(
        "rdps,spbw->drpbw", source_slot, got_rows, preferred_element_type=jnp.float32
    ).astype(jnp.bfloat16)
    source_all = source.reshape(num_panels, dev_lmos, dom_blocks, num_sets)
    tiles_in = got_tiles.reshape(num_sets, num_panels, dev_lmos, per_panel, BLK, BLK)
    strip_fock = jnp.einsum(
        "rdks,srdpab->drpakb", source_all, tiles_in, preferred_element_type=jnp.float32
    ).astype(jnp.bfloat16)
    strip_fock = strip_fock.reshape(dev_lmos, num_panels, per_panel, BLK, dom_width)
    fin_rows, fin_fock = (
        lax.all_to_all(strip_rows, "row", split_axis=1, concat_axis=1, tiled=True),
        lax.all_to_all(strip_fock, "row", split_axis=1, concat_axis=1, tiled=True),
    )
    fin_rows = fin_rows.reshape(dev_lmos, dom_width, row_width)
    fin_fock = fin_fock.reshape(dev_lmos, dom_width, dom_width)
    slot_rot = rotation[0]
    coef_dom = fin_rows[:, :, :occ_width]
    proj_dom = fin_rows[:, :, occ_width : 2 * occ_width]
    three_dom = fin_rows[:, :, 2 * occ_width :]
    fock_half = jnp.einsum(
        "dxy,dyn->dxn", fin_fock, slot_rot, preferred_element_type=jnp.float32
    ).astype(jnp.bfloat16)
    fock_rot = jnp.einsum("dxm,dxn->dmn", slot_rot, fock_half, preferred_element_type=jnp.float32)
    coef_rot = jnp.einsum(
        "dxm,dxi->dmi", slot_rot, coef_dom, preferred_element_type=jnp.float32
    ).astype(jnp.bfloat16)
    proj_rot = jnp.einsum(
        "dxm,dxi->dmi", slot_rot, proj_dom, preferred_element_type=jnp.float32
    ).astype(jnp.bfloat16)
    proj_fock = fock_rot - jnp.einsum(
        "dmi,dni->dmn", coef_rot, proj_rot, preferred_element_type=jnp.float32
    )
    proj_fock = proj_fock - jnp.einsum(
        "dmi,dni->dmn", proj_rot, coef_rot, preferred_element_type=jnp.float32
    )
    three_rot = jnp.einsum(
        "dxm,dxu->dmu", slot_rot, three_dom, preferred_element_type=jnp.float32
    ).astype(jnp.bfloat16)
    return (proj_fock[None], three_rot[None])


def solution(mesh):
    placed = (
        P("row", "col", None),
        P(("row", "col"), None),
        P(("row", "col"), None),
        P("col", "row", None, None),
        P(),
        P(),
    )
    return jax.shard_map(
        body,
        mesh=mesh,
        in_specs=placed,
        out_specs=(P("col", "row", None, None), P("col", "row", None, None)),
        check_vma=False,
    )
```

profile of v0, /device:TPU:1, one launch (start us, length us, event | category | flops | bytes accessed | tf_op | source)
XLA Modules:
  0.0 609.3 jit_solution(9066787770218420429)
XLA Ops:
  7.2 0.7 all-gather.2.cloned.1.call-update
  8.0 37.6 %all-gather.2.cloned.1.call-done = bf16[2048,1024]{1,0:T(8,128)(2,1)} async-done(((bf16[256,1024]{1,0:T(8,128)(2,1)}), bf16[2048,1024]{1,0:T(8,128)(2,1)}) %all-gather.2.cloned.1.call-update) | async-done | bytes 4194320 | tf_op jit(solution)/shard_map/all_gather | solution.py:29
  45.5 23.4 %fusion.5 = bf16[4096,1024]{1,0:T(8,128)(2,1)} fusion(bf16[2048,1024]{1,0:T(8,128)(2,1)} %all-gather.2.cloned.1.call-done, bf16[4096,1,2048]{2,0,1:T(8,128)(2,1)} %param.6), kind=kOutput, calls=%fused_computation.8 | convolution fusion | flops 17184063488 | bytes 29360128 | tf_op jit(solution)/shard_map/dot_general | solution.py:31
  69.0 9.7 %copy.120 = bf16[512,8,16,128]{3,2,1,0:T(8,128)(2,1)S(1)} copy(bf16[512,8,16,128]{3,1,2,0:T(8,128)(2,1)} %bitcast.129) | data formatting | bytes 33554432
  78.6 8.1 %copy.94 = bf16[32,128,16,128]{3,1,2,0:T(8,128)(2,1)} copy(bf16[32,128,16,128]{3,2,1,0:T(8,128)(2,1)S(1)} %bitcast.127) | data formatting | bytes 33554432 | tf_op jit(solution)/shard_map/reshape;squeeze | solution.py:47
  88.3 9.6 %gather_fusion.1 = bf16[128,128,128]{2,1,0:T(8,128)(2,1)} fusion(bf16[32,128,16,128]{3,1,2,0:T(8,128)(2,1)} %copy.94, s32[128]{0:T(128)S(1)} %reshape.172), kind=kCustom, calls=%fused_computation.1 | custom fusion | bytes 8389632 | tf_op jit(solution)/shard_map/gather | solution.py:68
  97.8 4.6 select_bitcast_fusion
  102.4 6.9 %all-to-all-start = ((bf16[16,8,1,128,128]{4,3,1,2,0:T(8,128)(2,1)}), bf16[16,8,1,128,128]{4,3,1,2,0:T(8,128)(2,1)}, u32[]{:S(2)}, u32[]{:S(2)}) async-start(bf16[16,8,1,128,128]{4,3,1,2,0:T(8,128)(2,1)} %select_bitcast_fusion), calls=%async_computation | async-start | bytes 8388608 | tf_op jit(solution)/shard_map/all_to_all | solution.py:72
  109.3 92.5 %reduce-scatter.2.cloned.1.call-done = bf16[256,1024]{1,0:T(8,128)(2,1)} async-done(((bf16[4096,1024]{1,0:T(8,128)(2,1)}), bf16[256,1024]{1,0:T(8,128)(2,1)}) %reduce-scatter.2.cloned.1.call-update) | async-done | bytes 524304 | tf_op jit(solution)/shard_map/reduce_scatter | solution.py:30
  201.8 3.7 convolution_bitcast_fusion
  205.5 104.6 %all-reduce.1 = bf16[1024,1024]{0,1:T(8,128)(2,1)} all-reduce(f32[1024,1024]{0,1:T(8,128)} %convolution_bitcast_fusion), channel_id=1, replica_groups=mesh['row'=8,'col'=16] {'row','col'}, use_global_device_ids=true, to_apply=%region_4.5 | all-reduce | flops 1048576 | bytes 6291456 | tf_op jit(solution)/shard_map/psum | solution.py:39
  310.2 2.4 fusion.36
  312.7 5.9 convert_bitcast_fusion
  318.6 13.7 %copy.105 = bf16[16,1,128,2560]{3,2,1,0:T(8,128)(2,1)} copy(bf16[16,1,128,2560]{3,0,2,1:T(8,128)(2,1)} %convert_bitcast_fusion) | data formatting | bytes 20971520 | tf_op jit(solution)/shard_map/convert_element_type | solution.py:67
  332.3 5.2 all-to-all-start.2
  338.0 4.6 convert_bitcast_fusion.1
  342.7 2.3 reshape.152
  345.0 144.6 %all-to-all-done.2 = bf16[16,1,128,2560]{3,2,1,0:T(8,128)(2,1)} async-done(((bf16[16,1,128,2560]{3,2,1,0:T(8,128)(2,1)}), bf16[16,1,128,2560]{3,2,1,0:T(8,128)(2,1)}, u32[]{:S(2)}, u32[]{:S(2)}) %all-to-all-start.2) | async-done | bytes 10485792 | tf_op jit(solution)/shard_map/all_to_all | solution.py:71
  489.5 9.3 %all-to-all-start.1 = ((bf16[1,8,1,128,1024]{4,3,2,0,1:T(8,128)(2,1)}), bf16[1,8,1,128,1024]{4,3,2,0,1:T(8,128)(2,1)S(1)}, u32[]{:S(2)}, u32[]{:S(2)}) async-start(bf16[1,8,1,128,1024]{4,3,2,0,1:T(8,128)(2,1)} %bitcast.16), calls=%async_computation.1 | async-start | bytes 4194304 | tf_op jit(solution)/shard_map/all_to_all | solution.py:88
  498.8 10.1 %fusion.11 = bf16[1,8,1,128,2560]{4,1,3,0,2:T(8,128)(2,1)S(1)} fusion(bf16[16,1,128,2560]{3,2,1,0:T(8,128)(2,1)} %all-to-all-done.2, pred[8,8,16]{2,0,1:T(8,128)(4,1)S(1)} %get-tuple-element.20, s32[]{:T(128)S(6)} %select_n.74), kind=kOutput, calls=%fused_computation.10 | convolution fusion | flops 86507520 | bytes 15729668 | tf_op jit(solution)/shard_map/rdps,spbw->drpbw/dot_general | solution.py:77
  508.9 3.8 copy.107
  512.8 12.4 %all-to-all-done.1 = bf16[1,8,1,128,1024]{4,3,2,0,1:T(8,128)(2,1)S(1)} async-done(((bf16[1,8,1,128,1024]{4,3,2,0,1:T(8,128)(2,1)}), bf16[1,8,1,128,1024]{4,3,2,0,1:T(8,128)(2,1)S(1)}, u32[]{:S(2)}, u32[]{:S(2)}) %all-to-all-start.1) | async-done | bytes 2097184 | tf_op jit(solution)/shard_map/all_to_all | solution.py:88
  525.2 5.4 all-to-all-start.3
  530.6 2.8 convolution_bitcast_fusion.1
  533.4 57.4 %all-to-all-done.3 = bf16[1,8,1,128,2560]{4,3,0,2,1:T(8,128)(2,1)} async-done(((bf16[1,8,1,128,2560]{4,3,0,2,1:T(8,128)(2,1)}), bf16[1,8,1,128,2560]{4,3,0,2,1:T(8,128)(2,1)}, u32[]{:S(2)}, u32[]{:S(2)}) %all-to-all-start.3) | async-done | bytes 5242912 | tf_op jit(solution)/shard_map/all_to_all | solution.py:87
  590.8 2.9 fusion.23
  593.6 2.9 fusion.24
  596.5 2.0 fusion.39
  598.6 0.8 convolution_subtract_fusion.1
  599.4 0.8 fusion.34
  600.1 1.3 copy.110
  601.4 1.0 copy.111
  (44 shorter events, 2.2 us)
Async XLA Ops:
  7.2 523.5 %copy-start = (bf16[1,1,1024,512]{3,2,1,0:T(8,128)(2,1)S(1)}, bf16[1,1,1024,512]{3,2,1,0:T(8,128)(2,1)}, u32[]{:S(2)}) copy-start(bf16[1,1,1024,512]{3,2,1,0:T(8,128)(2,1)} %param.9) | copy-start | bytes 3145732
  7.2 38.3 %all-gather.2.cloned.1.call-start = ((), (), s32[]{:S(2)}) async-start(), calls=%async_computation.5 | async-start | bytes 4718592 | tf_op jit(solution)/shard_map/all_gather | solution.py:29
  7.9 193.9 %reduce-scatter.2.cloned.1.call-start = ((), (), s32[]{:S(2)}) async-start(), calls=%async_computation.6 | async-start | bytes 8912896 | tf_op jit(solution)/shard_map/reduce_scatter | solution.py:30
  78.6 8.2 %copy-start.6 = (s32[128,8]{0,1:T(8,128)S(1)}, s32[128,8]{0,1:T(8,128)}, u32[]{:S(2)}) copy-start(s32[128,8]{0,1:T(8,128)} %param.11) | copy-start | bytes 12292
  78.6 8.3 %copy-start.5 = (s32[16,8]{0,1:T(8,128)S(1)}, s32[16,8]{0,1:T(8,128)}, u32[]{:S(2)}) copy-start(s32[16,8]{0,1:T(8,128)} %param.10) | copy-start | bytes 1540
  102.4 99.4 %copy-start.1 = (bf16[256,1024]{1,0:T(8,128)(2,1)S(1)}, bf16[256,1024]{1,0:T(8,128)(2,1)}, u32[]{:S(2)}) copy-start(bf16[256,1024]{1,0:T(8,128)(2,1)} %param.7) | copy-start | bytes 1572868
  102.4 229.9 %all-to-all-start = ((bf16[16,8,1,128,128]{4,3,1,2,0:T(8,128)(2,1)}), bf16[16,8,1,128,128]{4,3,1,2,0:T(8,128)(2,1)}, u32[]{:S(2)}, u32[]{:S(2)}) async-start(bf16[16,8,1,128,128]{4,3,1,2,0:T(8,128)(2,1)} %select_bitcast_fusion), calls=%async_computation | async-start | bytes 8388608 | tf_op jit(solution)/shard_map/all_to_all | solution.py:72
  205.5 104.7 %copy-start.2 = (bf16[256,1024]{1,0:T(8,128)(2,1)S(1)}, bf16[256,1024]{1,0:T(8,128)(2,1)}, u32[]{:S(2)}) copy-start(bf16[256,1024]{1,0:T(8,128)(2,1)} %reduce-scatter.2.cloned.1.call-done) | copy-start | bytes 1572868
  310.2 2.4 copy-start.4
  332.3 157.2 %all-to-all-start.2 = ((bf16[16,1,128,2560]{3,2,1,0:T(8,128)(2,1)}), bf16[16,1,128,2560]{3,2,1,0:T(8,128)(2,1)}, u32[]{:S(2)}, u32[]{:S(2)}) async-start(bf16[16,1,128,2560]{3,2,1,0:T(8,128)(2,1)} %copy.105), calls=%async_computation.3 | async-start | bytes 20971520 | tf_op jit(solution)/shard_map/all_to_all | solution.py:71
  489.5 35.7 %all-to-all-start.1 = ((bf16[1,8,1,128,1024]{4,3,2,0,1:T(8,128)(2,1)}), bf16[1,8,1,128,1024]{4,3,2,0,1:T(8,128)(2,1)S(1)}, u32[]{:S(2)}, u32[]{:S(2)}) async-start(bf16[1,8,1,128,1024]{4,3,2,0,1:T(8,128)(2,1)} %bitcast.16), calls=%async_computation.1 | async-start | bytes 4194304 | tf_op jit(solution)/shard_map/all_to_all | solution.py:88
  525.2 65.6 %all-to-all-start.3 = ((bf16[1,8,1,128,2560]{4,3,0,2,1:T(8,128)(2,1)}), bf16[1,8,1,128,2560]{4,3,0,2,1:T(8,128)(2,1)}, u32[]{:S(2)}, u32[]{:S(2)}) async-start(bf16[1,8,1,128,2560]{4,3,0,2,1:T(8,128)(2,1)} %copy.107), calls=%async_computation.4 | async-start | bytes 10485760 | tf_op jit(solution)/shard_map/all_to_all | solution.py:87
  596.5 2.1 copy-start.3
Sparse Core Ops, SparseCore 0:
  9.7 35.7 all-gather.1
  69.1 132.6 reduce-scatter.1
where the time goes:
time: 610 us; the launch traced here: 609 us
  waiting for transfers between devices  345 us (57%)
  blocking collectives  105 us (17%)
  matrix products  62.2 us (10%)
  local copies, waits for them, and re-layouts  51.2 us (8%)
  starting transfers between devices  26.9 us (4%)
  between operations  14.3 us (2%)
    all_to_all x1, waiting for transfers between devices, body(): lax.all_to_all(rows_out, 'col', split_axis=0, concat_axis=0, tiled=True)  145 us
    psum x1, blocking collectives, body(): occ_fock = lax.psum(occ_term, ('row', 'col'))  105 us
    reduce_scatter x1, waiting for transfers between devices, body(): lax.psum_scatter(jnp.dot(panel_fock, gathered, preferred_element_type=jnp...  92.5 us
    all_to_all x1, waiting for transfers between devices, body(): lax.all_to_all(strip_rows, 'row', split_axis=1, concat_axis=1, tiled=True)  57.4 us
    all_gather x1, waiting for transfers between devices, body(): gathered = lax.all_gather(lmo_coef, 'row', axis=0, tiled=True)  37.6 us
    dot_general x1, matrix products, body(): jnp.dot(panel_fock, gathered, preferred_element_type=jnp.float32)  23.4 us
    convert_element_type x1, local copies, waits for them, and re-layouts, body(): rows_out = jnp.einsum('ojps,sbw->opbw', pick_rows, row_blocks, preferred_...  13.7 us
    all_to_all x1, waiting for transfers between devices, body(): lax.all_to_all(strip_fock, 'row', split_axis=1, concat_axis=1, tiled=True)  12.4 us
  transfers between devices with their start and end apart: 6, of which 5 were waited for; matrix products, arithmetic and copies ran while one was open for 14% of the time, Pallas kernels for 0%

commit v1 on v0

--- a/solution.py
+++ b/solution.py
@@ -26,7 +26,9 @@
     dev_lmos = rotation.shape[1]
     dom_width = dom_blocks * BLK
     panel_fock = fock[:, 0, :]
-    gathered = lax.all_gather(lmo_coef, "row", axis=0, tiled=True)
+    gathered = jnp.concatenate(
+        lax.all_to_all(jnp.stack([lmo_coef] * lax.axis_size("row")), "row", 0, 0), axis=0
+    )
     fock_coef = lax.psum_scatter(
         jnp.dot(panel_fock, gathered, preferred_element_type=jnp.float32).astype(jnp.bfloat16),
         "col",

time: 610 us -> 638 us (1.046); the launches traced: 609 us -> 630 us
  blocking collectives: 105 us -> 160 us
  waiting for transfers between devices: 345 us -> 308 us
    all_to_all x0 -> x1, blocking collectives: none -> 55.1 us  [body(): lax.all_to_all(jnp.stack([lmo_coef] * lax.axis_size('row')), 'row', 0, 0)]
    all_gather x1 -> x0, waiting for transfers between devices: 37.6 us -> none  [body(): gathered = lax.all_gather(lmo_coef, 'row', axis=0, tiled=True)]
  transfers between devices with their start and end apart: 6 -> 5, of which waited for: 5 -> 4; matrix products, arithmetic and copies ran while one was open for 14% -> 13% of each run, Pallas kernels for 0% -> 0%
where the time goes in v1:
time: 638 us; the launch traced here: 630 us
  waiting for transfers between devices  308 us (48%)
  blocking collectives  160 us (25%)
  matrix products  61 us (10%)
  local copies, waits for them, and re-layouts  52.9 us (8%)
  starting transfers between devices  29.1 us (5%)
  between operations  14.5 us (2%)
    all_to_all x1, waiting for transfers between devices, body(): lax.all_to_all(rows_out, 'col', split_axis=0, concat_axis=0, tiled=True)  144 us
    psum x1, blocking collectives, body(): occ_fock = lax.psum(occ_term, ('row', 'col'))  105 us
    reduce_scatter x1, waiting for transfers between devices, body(): lax.psum_scatter(jnp.dot(panel_fock, gathered, preferred_element_type=jnp...  94.1 us
    all_to_all x1, waiting for transfers between devices, body(): lax.all_to_all(strip_rows, 'row', split_axis=1, concat_axis=1, tiled=True)  57.3 us
    all_to_all x1, blocking collectives, body(): lax.all_to_all(jnp.stack([lmo_coef] * lax.axis_size('row')), 'row', 0, 0)  55.1 us
    dot_general x1, matrix products, body(): jnp.dot(panel_fock, gathered, preferred_element_type=jnp.float32)  22.2 us
    convert_element_type x1, local copies, waits for them, and re-layouts, body(): rows_out = jnp.einsum('ojps,sbw->opbw', pick_rows, row_blocks, preferred_...  13.7 us
  transfers between devices with their start and end apart: 5, of which 4 were waited for; matrix products, arithmetic and copies ran while one was open for 13% of the time, Pallas kernels for 0%

profile of v1, /device:TPU:1, one launch (start us, length us, event | category | flops | bytes accessed | tf_op | source)
XLA Modules:
  0.0 630.4 jit_solution(10556257890780856384)
XLA Ops:
  7.2 1.6 stack.2
  8.9 55.1 %all_to_all.25 = bf16[8,256,1024]{2,1,0:T(8,128)(2,1)S(1)} all-to-all(bf16[8,256,1024]{2,1,0:T(8,128)(2,1)S(1)} %stack.2), channel_id=1, replica_groups=mesh['row'=8,'col'=16] {'row'}, dimensions={0} | all-to-all | bytes 8388608 | tf_op jit(solution)/shard_map/all_to_all | solution.py:30
  63.9 22.2 %fusion.5 = bf16[4096,1024]{1,0:T(8,128)(2,1)} fusion(bf16[2048,1024]{1,0:T(8,128)(2,1)S(1)} %bitcast.132, bf16[4096,1,2048]{2,0,1:T(8,128)(2,1)} %param.6), kind=kOutput, calls=%fused_computation.8 | convolution fusion | flops 17184063488 | bytes 29360128 | tf_op jit(solution)/shard_map/dot_general | solution.py:33
  86.1 9.7 %copy.120 = bf16[512,8,16,128]{3,2,1,0:T(8,128)(2,1)S(1)} copy(bf16[512,8,16,128]{3,1,2,0:T(8,128)(2,1)} %bitcast.130) | data formatting | bytes 33554432
  95.8 8.2 %copy.94 = bf16[32,128,16,128]{3,1,2,0:T(8,128)(2,1)} copy(bf16[32,128,16,128]{3,2,1,0:T(8,128)(2,1)S(1)} %bitcast.128) | data formatting | bytes 33554432 | tf_op jit(solution)/shard_map/reshape;squeeze | solution.py:49
  105.5 9.6 %gather_fusion.1 = bf16[128,128,128]{2,1,0:T(8,128)(2,1)} fusion(bf16[32,128,16,128]{3,1,2,0:T(8,128)(2,1)} %copy.94, s32[128]{0:T(128)S(1)} %reshape.178), kind=kCustom, calls=%fused_computation.1 | custom fusion | bytes 8389632 | tf_op jit(solution)/shard_map/gather | solution.py:70
  115.1 4.5 select_bitcast_fusion
  119.6 7.7 %all-to-all-start = ((bf16[16,8,1,128,128]{4,3,1,2,0:T(8,128)(2,1)}), bf16[16,8,1,128,128]{4,3,1,2,0:T(8,128)(2,1)}, u32[]{:S(2)}, u32[]{:S(2)}) async-start(bf16[16,8,1,128,128]{4,3,1,2,0:T(8,128)(2,1)} %select_bitcast_fusion), calls=%async_computation | async-start | bytes 8388608 | tf_op jit(solution)/shard_map/all_to_all | solution.py:74
  127.4 94.1 %reduce-scatter.2.cloned.1.call-done = bf16[256,1024]{1,0:T(8,128)(2,1)} async-done(((bf16[4096,1024]{1,0:T(8,128)(2,1)}), bf16[256,1024]{1,0:T(8,128)(2,1)}) %reduce-scatter.2.cloned.1.call-update) | async-done | bytes 524304 | tf_op jit(solution)/shard_map/reduce_scatter | solution.py:32
  221.5 3.7 convolution_bitcast_fusion
  225.2 104.6 %all-reduce.1 = bf16[1024,1024]{0,1:T(8,128)(2,1)} all-reduce(f32[1024,1024]{0,1:T(8,128)} %convolution_bitcast_fusion), channel_id=1, replica_groups=mesh['row'=8,'col'=16] {'row','col'}, use_global_device_ids=true, to_apply=%region_4.5 | all-reduce | flops 1048576 | bytes 6291456 | tf_op jit(solution)/shard_map/psum | solution.py:41
  329.8 2.4 fusion.36
  332.3 5.9 convert_bitcast_fusion
  338.2 13.7 %copy.105 = bf16[16,1,128,2560]{3,2,1,0:T(8,128)(2,1)} copy(bf16[16,1,128,2560]{3,0,2,1:T(8,128)(2,1)} %convert_bitcast_fusion) | data formatting | bytes 20971520 | tf_op jit(solution)/shard_map/convert_element_type | solution.py:69
  351.9 5.7 all-to-all-start.3
  358.2 4.6 convert_bitcast_fusion.1
  362.8 2.3 reshape.157
  365.1 144.5 %all-to-all-done.3 = bf16[16,1,128,2560]{3,2,1,0:T(8,128)(2,1)} async-done(((bf16[16,1,128,2560]{3,2,1,0:T(8,128)(2,1)}), bf16[16,1,128,2560]{3,2,1,0:T(8,128)(2,1)}, u32[]{:S(2)}, u32[]{:S(2)}) %all-to-all-start.3) | async-done | bytes 10485792 | tf_op jit(solution)/shard_map/all_to_all | solution.py:73
  509.6 10.0 %all-to-all-start.1 = ((bf16[1,8,1,128,1024]{4,3,2,0,1:T(8,128)(2,1)}), bf16[1,8,1,128,1024]{4,3,2,0,1:T(8,128)(2,1)S(1)}, u32[]{:S(2)}, u32[]{:S(2)}) async-start(bf16[1,8,1,128,1024]{4,3,2,0,1:T(8,128)(2,1)} %bitcast.16), calls=%async_computation.1 | async-start | bytes 4194304 | tf_op jit(solution)/shard_map/all_to_all | solution.py:90
  519.6 10.1 %fusion.11 = bf16[1,8,1,128,2560]{4,1,3,0,2:T(8,128)(2,1)S(1)} fusion(bf16[16,1,128,2560]{3,2,1,0:T(8,128)(2,1)} %all-to-all-done.3, pred[8,8,16]{2,0,1:T(8,128)(4,1)S(1)} %get-tuple-element.20, s32[]{:T(128)S(6)} %select_n.74), kind=kOutput, calls=%fused_computation.10 | convolution fusion | flops 86507520 | bytes 15729668 | tf_op jit(solution)/shard_map/rdps,spbw->drpbw/dot_general | solution.py:79
  529.6 3.8 copy.107
  533.5 12.4 %all-to-all-done.1 = bf16[1,8,1,128,1024]{4,3,2,0,1:T(8,128)(2,1)S(1)} async-done(((bf16[1,8,1,128,1024]{4,3,2,0,1:T(8,128)(2,1)}), bf16[1,8,1,128,1024]{4,3,2,0,1:T(8,128)(2,1)S(1)}, u32[]{:S(2)}, u32[]{:S(2)}) %all-to-all-start.1) | async-done | bytes 2097184 | tf_op jit(solution)/shard_map/all_to_all | solution.py:90
  545.9 5.7 all-to-all-start.4
  551.6 2.8 convolution_bitcast_fusion.1
  554.3 57.3 %all-to-all-done.4 = bf16[1,8,1,128,2560]{4,3,0,2,1:T(8,128)(2,1)} async-done(((bf16[1,8,1,128,2560]{4,3,0,2,1:T(8,128)(2,1)}), bf16[1,8,1,128,2560]{4,3,0,2,1:T(8,128)(2,1)}, u32[]{:S(2)}, u32[]{:S(2)}) %all-to-all-start.4) | async-done | bytes 5242912 | tf_op jit(solution)/shard_map/all_to_all | solution.py:89
  611.6 2.9 fusion.23
  614.5 2.9 fusion.24
  617.4 2.0 fusion.39
  619.5 0.8 convolution_subtract_fusion.1
  620.2 0.8 fusion.34
  621.0 1.3 copy.110
  622.3 1.0 copy.111
  (43 shorter events, 2.1 us)
Async XLA Ops:
  7.2 544.4 %copy-start = (bf16[1,1,1024,512]{3,2,1,0:T(8,128)(2,1)S(1)}, bf16[1,1,1024,512]{3,2,1,0:T(8,128)(2,1)}, u32[]{:S(2)}) copy-start(bf16[1,1,1024,512]{3,2,1,0:T(8,128)(2,1)} %param.9) | copy-start | bytes 3145732
  7.2 214.3 %reduce-scatter.2.cloned.1.call-start = ((), (), s32[]{:S(2)}) async-start(), calls=%async_computation.6 | async-start | bytes 8912896 | tf_op jit(solution)/shard_map/reduce_scatter | solution.py:32
  95.8 8.2 %copy-start.6 = (s32[128,8]{0,1:T(8,128)S(1)}, s32[128,8]{0,1:T(8,128)}, u32[]{:S(2)}) copy-start(s32[128,8]{0,1:T(8,128)} %param.11) | copy-start | bytes 12292
  95.8 8.3 %copy-start.5 = (s32[16,8]{0,1:T(8,128)S(1)}, s32[16,8]{0,1:T(8,128)}, u32[]{:S(2)}) copy-start(s32[16,8]{0,1:T(8,128)} %param.10) | copy-start | bytes 1540
  119.6 101.9 %copy-start.1 = (bf16[256,1024]{1,0:T(8,128)(2,1)S(1)}, bf16[256,1024]{1,0:T(8,128)(2,1)}, u32[]{:S(2)}) copy-start(bf16[256,1024]{1,0:T(8,128)(2,1)} %param.7) | copy-start | bytes 1572868
  119.6 232.3 %all-to-all-start = ((bf16[16,8,1,128,128]{4,3,1,2,0:T(8,128)(2,1)}), bf16[16,8,1,128,128]{4,3,1,2,0:T(8,128)(2,1)}, u32[]{:S(2)}, u32[]{:S(2)}) async-start(bf16[16,8,1,128,128]{4,3,1,2,0:T(8,128)(2,1)} %select_bitcast_fusion), calls=%async_computation | async-start | bytes 8388608 | tf_op jit(solution)/shard_map/all_to_all | solution.py:74
  225.2 104.6 %copy-start.2 = (bf16[256,1024]{1,0:T(8,128)(2,1)S(1)}, bf16[256,1024]{1,0:T(8,128)(2,1)}, u32[]{:S(2)}) copy-start(bf16[256,1024]{1,0:T(8,128)(2,1)} %reduce-scatter.2.cloned.1.call-done) | copy-start | bytes 1572868
  329.8 2.4 copy-start.4
  351.9 157.6 %all-to-all-start.3 = ((bf16[16,1,128,2560]{3,2,1,0:T(8,128)(2,1)}), bf16[16,1,128,2560]{3,2,1,0:T(8,128)(2,1)}, u32[]{:S(2)}, u32[]{:S(2)}) async-start(bf16[16,1,128,2560]{3,2,1,0:T(8,128)(2,1)} %copy.105), calls=%async_computation.4 | async-start | bytes 20971520 | tf_op jit(solution)/shard_map/all_to_all | solution.py:73
  509.6 36.3 %all-to-all-start.1 = ((bf16[1,8,1,128,1024]{4,3,2,0,1:T(8,128)(2,1)}), bf16[1,8,1,128,1024]{4,3,2,0,1:T(8,128)(2,1)S(1)}, u32[]{:S(2)}, u32[]{:S(2)}) async-start(bf16[1,8,1,128,1024]{4,3,2,0,1:T(8,128)(2,1)} %bitcast.16), calls=%async_computation.1 | async-start | bytes 4194304 | tf_op jit(solution)/shard_map/all_to_all | solution.py:90
  545.9 65.8 %all-to-all-start.4 = ((bf16[1,8,1,128,2560]{4,3,0,2,1:T(8,128)(2,1)}), bf16[1,8,1,128,2560]{4,3,0,2,1:T(8,128)(2,1)}, u32[]{:S(2)}, u32[]{:S(2)}) async-start(bf16[1,8,1,128,2560]{4,3,0,2,1:T(8,128)(2,1)} %copy.107), calls=%async_computation.5 | async-start | bytes 10485760 | tf_op jit(solution)/shard_map/all_to_all | solution.py:89
  617.4 2.1 copy-start.3
Sparse Core Ops, SparseCore 0:
  86.3 135.1 reduce-scatter.1
